TPU v7x, 512 devices: a whole 4x4x16 slice. The times are simulated.
512 devices in a mesh: dp: 32 (over x, y, core), expert: 16 (over z).
Axes of the slice: x: 4, y: 4, z: 16, core: 2. Of those that a mesh axis runs over, the one named last changes fastest.
Arguments:
- out_grad: bfloat16 [65536, 2048], P(('dp', 'expert')), may hold values from -6 to 6
- expert_ids: int32 [65536, 4], P(('dp', 'expert')), may hold values from 0 to 15, all different within a row; in each aligned block of 128 rows (0 to 127, 128 to 255, ...) at most 64 rows name the same one
- route_weights: bfloat16 [65536, 4], P(('dp', 'expert')), may hold values from 0.049804688 to 1
- pre_activations: bfloat16 [65536, 4, 1536], P(('dp', 'expert')), may hold values from -6 to 6
- down_weight: bfloat16 [16, 768, 2048], P('expert', 'dp'), may hold values from -0.21875 to 0.21875
Outputs:
- pre_grad: bfloat16 [65536, 4, 1536], P(('dp', 'expert'))
- weight_grad: bfloat16 [65536, 4], P(('dp', 'expert'))
- down_grad: bfloat16 [16, 768, 2048], P('expert', 'dp')
Inputs may be any that keep to these rules, and one draw needn't show every extreme that they name: `expert_ids`: among the 128 rows of one device, each expert is named by at most 64 rows, a bound that some block reaches; the numbers in a row are distinct.
All inputs are finite; a program needn't handle non-finite values.
Results may differ from a plain program's by a relative error of at most 0.015.
Values may be sent and summed in bfloat16 or wider, within the bound.
No kernel may reach another device: no remote copies, remote signals or barrier semaphores. Data moves between devices by JAX's collectives and lax.ppermute only.
A program may use at most 64 MiB of HBM per device.

v0:
```python
import jax
import jax.numpy as jnp
from jax import lax
from jax.sharding import PartitionSpec as P

F32 = jnp.float32
BF16 = jnp.bfloat16


def gather_rows(x):
    return lax.all_gather(x, "dp", axis=0, tiled=True)


def body(out_grad, expert_ids, route_weights, pre_activations, down_weight):
    tok, width = out_grad.shape
    top = expert_ids.shape[1]
    units = pre_activations.shape[2] // 2
    ndp = lax.axis_size("dp")
    rows = down_weight.shape[1]
    n_all = ndp * tok
    w_all = lax.all_gather(down_weight, "expert", axis=0, tiled=True)
    experts = w_all.shape[0]
    wcat = w_all.reshape(experts * rows, width)
    og_all = gather_rows(out_grad)
    ids_t = gather_rows(expert_ids).T
    rw_t = gather_rows(route_weights).T.astype(F32)
    gate = pre_activations[..., :units].astype(F32)
    up = pre_activations[..., units:].astype(F32)
    sig = jax.nn.sigmoid(gate)
    hidden = (gate * sig * up).astype(BF16)
    send_h = hidden.reshape(tok, top, ndp, rows).transpose(2, 0, 1, 3)
    got_h = lax.all_to_all(send_h, "dp", 0, 0, tiled=True)
    hid_t = got_h.transpose(2, 3, 0, 1).reshape(top, rows, n_all).astype(F32)
    eidx = jnp.arange(experts, dtype=jnp.int32)[:, None, None]
    hp = jnp.zeros((experts, rows, n_all), F32)
    for k in range(top):
        hp = hp + jnp.where(
            ids_t[k][None, None, :] == eidx, (rw_t[k][None, :] * hid_t[k])[None], 0.0
        )
    hp = hp.reshape(experts * rows, n_all).astype(BF16)
    part = lax.dot_general(hp, og_all, (((1,), (0,)), ((), ())), preferred_element_type=F32)
    r_t = lax.dot_general(wcat, og_all, (((1,), (1,)), ((), ())), preferred_element_type=F32)
    r_t = r_t.reshape(experts, rows, n_all)
    hg_t = jnp.stack(
        [jnp.sum(jnp.where(ids_t[k][None, None, :] == eidx, r_t, 0.0), axis=0) for k in range(top)]
    ).astype(BF16)
    send_g = hg_t.reshape(top, rows, ndp, tok).transpose(2, 3, 0, 1)
    got_g = lax.all_to_all(send_g, "dp", 0, 0, tiled=True)
    hidden_grad = got_g.transpose(1, 2, 0, 3).reshape(tok, top, units)
    hg32 = hidden_grad.astype(F32)
    weight_grad = jnp.sum(hg32 * hidden.astype(F32), axis=-1).astype(BF16)
    cot = route_weights.astype(F32)[..., None] * hg32
    gate_grad = cot * up * sig * (1.0 + gate * (1.0 - sig))
    up_grad = cot * gate * sig
    pre_grad = jnp.concatenate([gate_grad, up_grad], axis=-1).astype(BF16)
    summed = lax.psum_scatter(
        part.reshape(experts, rows, width).astype(BF16), "expert", scatter_dimension=0, tiled=True
    )
    down_grad = (summed.astype(F32) / ndp).astype(BF16)
    return (pre_grad, weight_grad, down_grad)


def solution(mesh):
    return jax.shard_map(
        body,
        mesh=mesh,
        in_specs=(
            P(("dp", "expert"), None),
            P(("dp", "expert"), None),
            P(("dp", "expert"), None),
            P(("dp", "expert"), None, None),
            P("expert", "dp", None),
        ),
        out_specs=(
            P(("dp", "expert"), None, None),
            P(("dp", "expert"), None),
            P("expert", "dp", None),
        ),
        check_vma=False,
    )
```

profile of v0, /device:TPU:4, one launch (start us, length us, event | category | flops | bytes accessed | tf_op | source)
XLA Modules:
  0.0 325.2 jit_solution(932634305599170821)
XLA Ops:
  7.2 0.7 all-gather.3.cloned.1.call-update
  7.9 0.7 all-gather.5.cloned.1.call-update
  8.6 1.9 fusion.30
  10.6 0.7 copy.37
  11.3 0.7 copy.36
  12.0 24.4 %all_gather.15 = bf16[4096,4]{0,1:T(4,128)(2,1)S(1)} all-gather(bf16[128,4]{0,1:T(4,128)(2,1)S(1)} %copy-done.1), channel_id=1, replica_groups=mesh['dp'=32,'expert'=16] {'dp'}, dimensions={0}, use_global_device_ids=true | all-gather | bytes 33792 | tf_op jit(solution)/shard_map/all_gather | solution.py:11
  36.4 24.9 %all_gather.12 = s32[4096,4]{0,1:T(4,128)S(1)} all-gather(s32[128,4]{0,1:T(4,128)S(1)} %copy-done.2), channel_id=1, replica_groups=mesh['dp'=32,'expert'=16] {'dp'}, dimensions={0}, use_global_device_ids=true | all-gather | bytes 67584 | tf_op jit(solution)/shard_map/all_gather | solution.py:11
  61.5 24.7 %all-gather.3.cloned.1.call-done = bf16[16,24,2048]{2,1,0:T(8,128)(2,1)} async-done(((bf16[1,24,2048]{2,1,0:T(8,128)(2,1)}), bf16[16,24,2048]{2,1,0:T(8,128)(2,1)}) %all-gather.3.cloned.1.call-update) | async-done | bytes 1572880 | tf_op jit(solution)/shard_map/all_gather | solution.py:21
  86.3 88.2 %all-gather.5.cloned.1.call-done = bf16[4096,2048]{1,0:T(8,128)(2,1)} async-done(((bf16[128,2048]{1,0:T(8,128)(2,1)}), bf16[4096,2048]{1,0:T(8,128)(2,1)}) %all-gather.5.cloned.1.call-update) | async-done | bytes 16777232 | tf_op jit(solution)/shard_map/all_gather | solution.py:11
  174.5 12.7 %select_reduce_fusion.3 = (bf16[24,4096]{1,0:T(8,128)(2,1)S(1)}, bf16[24,4096]{1,0:T(8,128)(2,1)S(1)}, bf16[24,4096]{1,0:T(8,128)(2,1)S(1)}, bf16[24,4096]{1,0:T(8,128)(2,1)S(1)}) fusion(pred[16,4096]{1,0:T(8,128)(4,1)S(1)} %get-tuple-element.37, pred[16,4096]{1,0:T(8,128)(4,1)S(1)} %get-tuple-element.34, pred[16,4096]{1,0:T(8,128)(4,1)S(1)} %get-tuple-element.35, ...), kind=kOutput, calls=%fused_computation.8 | convolution fusion | flops 6454640640 | bytes 19398656 | tf_op jit(solution)/shard_map/dot_general | solution.py:42
  187.5 1.2 copy.25
  188.7 5.7 %all-to-all-start = ((bf16[32,128,4,24]{1,3,2,0:T(8,128)(2,1)}), bf16[32,128,4,24]{1,3,2,0:T(8,128)(2,1)S(1)}, u32[]{:S(2)}, u32[]{:S(2)}) async-start(bf16[32,128,4,24]{1,3,2,0:T(8,128)(2,1)} %copy.25), calls=%async_computation | async-start | bytes 1572864 | tf_op jit(solution)/shard_map/all_to_all | solution.py:48
  194.4 12.1 %all-to-all-done = bf16[32,128,4,24]{1,3,2,0:T(8,128)(2,1)S(1)} async-done(((bf16[32,128,4,24]{1,3,2,0:T(8,128)(2,1)}), bf16[32,128,4,24]{1,3,2,0:T(8,128)(2,1)S(1)}, u32[]{:S(2)}, u32[]{:S(2)}) %all-to-all-start) | async-done | bytes 786464 | tf_op jit(solution)/shard_map/all_to_all | solution.py:48
  206.5 2.6 fusion.26
  209.1 1.0 copy.29
  210.1 5.9 %all-to-all-start.1 = ((bf16[32,128,4,24]{1,3,2,0:T(8,128)(2,1)}), bf16[32,128,4,24]{1,3,2,0:T(8,128)(2,1)S(1)}, u32[]{:S(2)}, u32[]{:S(2)}) async-start(bf16[32,128,4,24]{1,3,2,0:T(8,128)(2,1)} %copy.29), calls=%async_computation.1 | async-start | bytes 1572864 | tf_op jit(solution)/shard_map/all_to_all | solution.py:32
  216.0 0.2 reduce-scatter.2.cloned.1.call-start
  216.3 11.8 %all-to-all-done.1 = bf16[32,128,4,24]{1,3,2,0:T(8,128)(2,1)S(1)} async-done(((bf16[32,128,4,24]{1,3,2,0:T(8,128)(2,1)}), bf16[32,128,4,24]{1,3,2,0:T(8,128)(2,1)S(1)}, u32[]{:S(2)}, u32[]{:S(2)}) %all-to-all-start.1) | async-done | bytes 786464 | tf_op jit(solution)/shard_map/all_to_all | solution.py:32
  228.1 0.3 convert_bitcast_fusion
  228.5 0.3 broadcast_multiply_fusion
  228.8 0.2 copy.50
  229.1 0.3 broadcast_multiply_fusion.1
  229.4 0.2 copy.51
  229.6 0.3 broadcast_multiply_fusion.2
  229.9 0.2 copy.52
  230.2 0.3 broadcast_multiply_fusion.3
  230.5 0.2 copy.53
  230.8 13.7 %fusion.13 = bf16[16,24,2048]{2,1,0:T(8,128)(2,1)} fusion(bf16[4096,2048]{1,0:T(8,128)(2,1)} %all-gather.5.cloned.1.call-done, f32[24,4096]{1,0:T(8,128)S(1)} %bitcast.84, f32[24,4096]{1,0:T(8,128)S(1)} %bitcast.85, f32[24,4096]{1,0:T(8,128)S(1)} %bitcast.86, f32[24,4096]{1,0:T(8,128)S(1)} %bitcast.87, pred[16,4096]{1,0:T(8,128)(4,1)S(1)} %get-tuple-element.34, ...), kind=kOutput, calls=%fused_computation.18 | convolution fusion | flops 6455820288 | bytes 20185088 | tf_op jit(solution)/shard_map/dot_general | solution.py:41
  244.5 1.1 copy-done
  245.7 2.5 copy.31
  248.2 69.0 %reduce-scatter.2.cloned.1.call-done = bf16[1,24,2048]{2,1,0:T(8,128)(2,1)} async-done(((bf16[16,24,2048]{2,1,0:T(8,128)(2,1)}), bf16[1,24,2048]{2,1,0:T(8,128)(2,1)}) %reduce-scatter.2.cloned.1.call-update) | async-done | bytes 98320 | tf_op jit(solution)/shard_map/reduce_scatter | solution.py:56
  317.1 1.6 multiply_convert_fusion
  (21 shorter events, 0.8 us)
Async XLA Ops:
  7.2 79.1 %all-gather.3.cloned.1.call-start = ((), (), s32[]{:S(2)}) async-start(), calls=%async_computation.3 | async-start | bytes 1671168 | tf_op jit(solution)/shard_map/all_gather | solution.py:21
  7.9 166.6 %all-gather.5.cloned.1.call-start = ((), (), s32[]{:S(2)}) async-start(), calls=%async_computation.4 | async-start | bytes 17301504 | tf_op jit(solution)/shard_map/all_gather | solution.py:11
  10.6 1.4 copy-start.1
  10.6 25.8 %copy-start.2 = (s32[128,4]{0,1:T(4,128)S(1)}, s32[128,4]{0,1:T(4,128)}, u32[]{:S(2)}) copy-start(s32[128,4]{0,1:T(4,128)} %param.6) | copy-start | bytes 6148
  188.7 17.8 %all-to-all-start = ((bf16[32,128,4,24]{1,3,2,0:T(8,128)(2,1)}), bf16[32,128,4,24]{1,3,2,0:T(8,128)(2,1)S(1)}, u32[]{:S(2)}, u32[]{:S(2)}) async-start(bf16[32,128,4,24]{1,3,2,0:T(8,128)(2,1)} %copy.25), calls=%async_computation | async-start | bytes 1572864 | tf_op jit(solution)/shard_map/all_to_all | solution.py:48
  210.1 18.0 %all-to-all-start.1 = ((bf16[32,128,4,24]{1,3,2,0:T(8,128)(2,1)}), bf16[32,128,4,24]{1,3,2,0:T(8,128)(2,1)S(1)}, u32[]{:S(2)}, u32[]{:S(2)}) async-start(bf16[32,128,4,24]{1,3,2,0:T(8,128)(2,1)} %copy.29), calls=%async_computation.1 | async-start | bytes 1572864 | tf_op jit(solution)/shard_map/all_to_all | solution.py:32
  216.0 101.1 %reduce-scatter.2.cloned.1.call-start = ((), (), s32[]{:S(2)}) async-start(), calls=%async_computation.5 | async-start | bytes 1671168 | tf_op jit(solution)/shard_map/reduce_scatter | solution.py:56
  244.4 1.1 copy-start
Sparse Core Ops, SparseCore 0:
  10.1 76.1 all-gather.2
  89.4 85.0 all-gather.4
  244.6 72.4 reduce-scatter.1
where the time goes:
time: 326 us; the launch traced here: 325 us
  waiting for transfers between devices  207 us (63%)
  blocking collectives  49.4 us (15%)
  matrix products  26.4 us (8%)
  between operations  14 us (4%)
  starting transfers between devices  11.9 us (4%)
  local copies, waits for them, and re-layouts  10.3 us (3%)
  other arithmetic  6.07 us (2%)
    all_gather x1, waiting for transfers between devices, gather_rows(): return lax.all_gather(x, 'dp', axis=0, tiled=True)  88.2 us
    reduce_scatter x1, waiting for transfers between devices, body(): lax.psum_scatter(part.reshape(experts, rows, width).astype(BF16), 'expert...  69 us
    all_gather x2, blocking collectives, gather_rows(): return lax.all_gather(x, 'dp', axis=0, tiled=True)  49.4 us
    all_gather x1, waiting for transfers between devices, body(): w_all = lax.all_gather(down_weight, 'expert', axis=0, tiled=True)  24.7 us
    dot_general x1, matrix products, body(): lax.dot_general(hp, og_all, (((1,), (0,)), ((), ())), preferred_element_t...  13.7 us
    dot_general x1, matrix products, body(): lax.dot_general(wcat, og_all, (((1,), (1,)), ((), ())), preferred_element...  12.7 us
    all_to_all x1, waiting for transfers between devices, body(): got_g = lax.all_to_all(send_g, 'dp', 0, 0, tiled=True)  12.1 us
    all_to_all x1, waiting for transfers between devices, body(): got_h = lax.all_to_all(send_h, 'dp', 0, 0, tiled=True)  11.8 us
  transfers between devices with their start and end apart: 5, of which 5 were waited for; matrix products, arithmetic and copies ran while one was open for 2% of the time, Pallas kernels for 0%

commit v1 on v0

--- a/solution.py
+++ b/solution.py
@@ -18,7 +18,9 @@
     ndp = lax.axis_size("dp")
     rows = down_weight.shape[1]
     n_all = ndp * tok
-    w_all = lax.all_gather(down_weight, "expert", axis=0, tiled=True)
+    w_all = jnp.concatenate(
+        lax.all_to_all(jnp.stack([down_weight] * lax.axis_size("expert")), "expert", 0, 0), axis=0
+    )
     experts = w_all.shape[0]
     wcat = w_all.reshape(experts * rows, width)
     og_all = gather_rows(out_grad)

time: 326 us -> 255 us (0.78)
  waiting for transfers between devices: 207 us -> 121 us
  starting transfers between devices: 11.9 us -> 27.1 us
    all_gather x1, waiting for transfers between devices: 88.2 us -> 3.93 us  [gather_rows(): return lax.all_gather(x, 'dp', axis=0, tiled=True)]
    all_gather x1 -> x0, waiting for transfers between devices: 24.7 us -> none  [body(): w_all = lax.all_gather(down_weight, 'expert', axis=0, tiled=True)]
    all_to_all x0 -> x1, waiting for transfers between devices: none -> 23.6 us  [body(): lax.all_to_all(jnp.stack([down_weight] * lax.axis_size('expert')), 'exper...]
    all_to_all x0 -> x1, starting transfers between devices: none -> 15.2 us  [body(): lax.all_to_all(jnp.stack([down_weight] * lax.axis_size('expert')), 'exper...]
  transfers between devices with their start and end apart: 5 -> 5, of which waited for: 5 -> 5; matrix products, arithmetic and copies ran while one was open for 2% -> 3% of each run, Pallas kernels for 0% -> 0%
where the time goes in v1:
time: 255 us
  waiting for transfers between devices  121 us (47%)
  blocking collectives  47.2 us (19%)
  starting transfers between devices  27.1 us (11%)
  matrix products  26.4 us (10%)
  between operations  14.3 us (6%)
  local copies, waits for them, and re-layouts  12.5 us (5%)
  other arithmetic  6.07 us (2%)
    reduce_scatter x1, waiting for transfers between devices, body(): lax.psum_scatter(part.reshape(experts, rows, width).astype(BF16), 'expert...  69 us
    all_gather x2, blocking collectives, gather_rows(): return lax.all_gather(x, 'dp', axis=0, tiled=True)  47.2 us
    all_to_all x1, waiting for transfers between devices, body(): lax.all_to_all(jnp.stack([down_weight] * lax.axis_size('expert')), 'exper...  23.6 us
    all_to_all x1, starting transfers between devices, body(): lax.all_to_all(jnp.stack([down_weight] * lax.axis_size('expert')), 'exper...  15.2 us
    dot_general x1, matrix products, body(): lax.dot_general(hp, og_all, (((1,), (0,)), ((), ())), preferred_element_t...  13.6 us
    dot_general x1, matrix products, body(): lax.dot_general(wcat, og_all, (((1,), (1,)), ((), ())), preferred_element...  12.7 us
    all_to_all x1, waiting for transfers between devices, body(): got_g = lax.all_to_all(send_g, 'dp', 0, 0, tiled=True)  12.1 us
    all_to_all x1, waiting for transfers between devices, body(): got_h = lax.all_to_all(send_h, 'dp', 0, 0, tiled=True)  11.8 us
  transfers between devices with their start and end apart: 5, of which 5 were waited for; matrix products, arithmetic and copies ran while one was open for 3% of the time, Pallas kernels for 0%

profile of v1, /device:TPU:4, one launch (start us, length us, event | category | flops | bytes accessed | tf_op | source)
XLA Modules:
  0.0 254.6 jit_solution(1721709328803460538)
XLA Ops:
  7.2 0.7 all-gather.2.cloned.1.call-update
  7.9 2.2 stack.12
  10.1 15.2 %all-to-all-start = ((bf16[16,1,24,2048]{3,2,1,0:T(8,128)(2,1)}), bf16[16,1,24,2048]{3,2,1,0:T(8,128)(2,1)}, u32[]{:S(2)}, u32[]{:S(2)}) async-start(bf16[16,1,24,2048]{3,2,1,0:T(8,128)(2,1)} %stack.12), calls=%async_computation | async-start | bytes 3145728 | tf_op jit(solution)/shard_map/all_to_all | solution.py:22
  25.4 1.9 fusion.31
  27.3 0.7 copy.37
  28.0 0.7 copy.36
  28.7 23.1 %all_gather.11 = bf16[4096,4]{0,1:T(4,128)(2,1)S(1)} all-gather(bf16[128,4]{0,1:T(4,128)(2,1)S(1)} %copy-done.1), channel_id=1, replica_groups=mesh['dp'=32,'expert'=16] {'dp'}, dimensions={0}, use_global_device_ids=true | all-gather | bytes 33792 | tf_op jit(solution)/shard_map/all_gather | solution.py:11
  51.8 24.0 %all_gather.9 = s32[4096,4]{0,1:T(4,128)S(1)} all-gather(s32[128,4]{0,1:T(4,128)S(1)} %copy-done.2), channel_id=1, replica_groups=mesh['dp'=32,'expert'=16] {'dp'}, dimensions={0}, use_global_device_ids=true | all-gather | bytes 67584 | tf_op jit(solution)/shard_map/all_gather | solution.py:11
  76.1 23.6 %all-to-all-done = bf16[16,1,24,2048]{3,2,1,0:T(8,128)(2,1)} async-done(((bf16[16,1,24,2048]{3,2,1,0:T(8,128)(2,1)}), bf16[16,1,24,2048]{3,2,1,0:T(8,128)(2,1)}, u32[]{:S(2)}, u32[]{:S(2)}) %all-to-all-start) | async-done | bytes 1572896 | tf_op jit(solution)/shard_map/all_to_all | solution.py:22
  99.7 3.9 %all-gather.2.cloned.1.call-done = bf16[4096,2048]{1,0:T(8,128)(2,1)} async-done(((bf16[128,2048]{1,0:T(8,128)(2,1)}), bf16[4096,2048]{1,0:T(8,128)(2,1)}) %all-gather.2.cloned.1.call-update) | async-done | bytes 16777232 | tf_op jit(solution)/shard_map/all_gather | solution.py:11
  103.6 12.7 %select_reduce_fusion.3 = (bf16[24,4096]{1,0:T(8,128)(2,1)S(1)}, bf16[24,4096]{1,0:T(8,128)(2,1)S(1)}, bf16[24,4096]{1,0:T(8,128)(2,1)S(1)}, bf16[24,4096]{1,0:T(8,128)(2,1)S(1)}) fusion(pred[16,4096]{1,0:T(8,128)(4,1)S(1)} %get-tuple-element.37, pred[16,4096]{1,0:T(8,128)(4,1)S(1)} %get-tuple-element.34, pred[16,4096]{1,0:T(8,128)(4,1)S(1)} %get-tuple-element.35, ...), kind=kOutput, calls=%fused_computation.8 | convolution fusion | flops 6454640640 | bytes 19398656 | tf_op jit(solution)/shard_map/dot_general | solution.py:44
  116.6 1.2 copy.25
  117.8 5.7 %all-to-all-start.1 = ((bf16[32,128,4,24]{1,3,2,0:T(8,128)(2,1)}), bf16[32,128,4,24]{1,3,2,0:T(8,128)(2,1)S(1)}, u32[]{:S(2)}, u32[]{:S(2)}) async-start(bf16[32,128,4,24]{1,3,2,0:T(8,128)(2,1)} %copy.25), calls=%async_computation.1 | async-start | bytes 1572864 | tf_op jit(solution)/shard_map/all_to_all | solution.py:50
  123.5 12.1 %all-to-all-done.1 = bf16[32,128,4,24]{1,3,2,0:T(8,128)(2,1)S(1)} async-done(((bf16[32,128,4,24]{1,3,2,0:T(8,128)(2,1)}), bf16[32,128,4,24]{1,3,2,0:T(8,128)(2,1)S(1)}, u32[]{:S(2)}, u32[]{:S(2)}) %all-to-all-start.1) | async-done | bytes 786464 | tf_op jit(solution)/shard_map/all_to_all | solution.py:50
  135.6 2.6 %fusion.26 = (bf16[128,4]{0,1:T(4,128)(2,1)}, bf16[128,4,768]{0,2,1:T(8,128)(2,1)S(1)}, bf16[128,4,768]{0,2,1:T(8,128)(2,1)S(1)}, bf16[128,4,768]{0,2,1:T(8,128)(2,1)}) fusion(bf16[32,128,4,24]{1,3,2,0:T(8,128)(2,1)S(1)} %all-to-all-done.1, bf16[128,4,768]{0,2,1:T(8,128)(2,1)S(1)} %copy.37, bf16[128,4,768]{0,2,1:T(8,128)(2,1)S(1)} %copy.36, ...), kind=kLoop, calls=%fused_computation.38 | loop fusion | flops 9043456 | bytes 4721664 | tf_op jit(solution)/shard_map/reduce_sum | solution.py:53
  138.2 1.0 copy.29
  139.2 5.9 %all-to-all-start.2 = ((bf16[32,128,4,24]{1,3,2,0:T(8,128)(2,1)}), bf16[32,128,4,24]{1,3,2,0:T(8,128)(2,1)S(1)}, u32[]{:S(2)}, u32[]{:S(2)}) async-start(bf16[32,128,4,24]{1,3,2,0:T(8,128)(2,1)} %copy.29), calls=%async_computation.2 | async-start | bytes 1572864 | tf_op jit(solution)/shard_map/all_to_all | solution.py:34
  145.4 11.8 %all-to-all-done.2 = bf16[32,128,4,24]{1,3,2,0:T(8,128)(2,1)S(1)} async-done(((bf16[32,128,4,24]{1,3,2,0:T(8,128)(2,1)}), bf16[32,128,4,24]{1,3,2,0:T(8,128)(2,1)S(1)}, u32[]{:S(2)}, u32[]{:S(2)}) %all-to-all-start.2) | async-done | bytes 786464 | tf_op jit(solution)/shard_map/all_to_all | solution.py:34
  157.2 0.3 convert_bitcast_fusion
  157.6 0.3 broadcast_multiply_fusion
  157.9 0.2 copy.50
  158.2 0.3 broadcast_multiply_fusion.1
  158.5 0.2 copy.51
  158.7 0.3 broadcast_multiply_fusion.2
  159.1 0.2 copy.52
  159.3 0.3 broadcast_multiply_fusion.3
  159.6 0.2 copy.53
  159.9 13.6 %fusion.13 = bf16[16,24,2048]{2,1,0:T(8,128)(2,1)} fusion(bf16[4096,2048]{1,0:T(8,128)(2,1)} %all-gather.2.cloned.1.call-done, f32[24,4096]{1,0:T(8,128)S(1)} %bitcast.89, f32[24,4096]{1,0:T(8,128)S(1)} %bitcast.90, f32[24,4096]{1,0:T(8,128)S(1)} %bitcast.91, f32[24,4096]{1,0:T(8,128)S(1)} %bitcast.92, pred[16,4096]{1,0:T(8,128)(4,1)S(1)} %get-tuple-element.34, ...), kind=kOutput, calls=%fused_computation.18 | convolution fusion | flops 6455820288 | bytes 20185088 | tf_op jit(solution)/shard_map/dot_general | solution.py:43
  173.5 1.1 copy-done
  174.7 2.5 copy.31
  177.2 69.0 %reduce-scatter.2.cloned.1.call-done = bf16[1,24,2048]{2,1,0:T(8,128)(2,1)} async-done(((bf16[16,24,2048]{2,1,0:T(8,128)(2,1)}), bf16[1,24,2048]{2,1,0:T(8,128)(2,1)}) %reduce-scatter.2.cloned.1.call-update) | async-done | bytes 98320 | tf_op jit(solution)/shard_map/reduce_scatter | solution.py:58
  246.2 1.6 multiply_convert_fusion
  (21 shorter events, 1.0 us)
Async XLA Ops:
  7.2 96.4 %all-gather.2.cloned.1.call-start = ((), (), s32[]{:S(2)}) async-start(), calls=%async_computation.4 | async-start | bytes 17301504 | tf_op jit(solution)/shard_map/all_gather | solution.py:11
  10.1 89.5 %all-to-all-start = ((bf16[16,1,24,2048]{3,2,1,0:T(8,128)(2,1)}), bf16[16,1,24,2048]{3,2,1,0:T(8,128)(2,1)}, u32[]{:S(2)}, u32[]{:S(2)}) async-start(bf16[16,1,24,2048]{3,2,1,0:T(8,128)(2,1)} %stack.12), calls=%async_computation | async-start | bytes 3145728 | tf_op jit(solution)/shard_map/all_to_all | solution.py:22
  27.3 1.4 copy-start.1
  27.3 24.5 %copy-start.2 = (s32[128,4]{0,1:T(4,128)S(1)}, s32[128,4]{0,1:T(4,128)}, u32[]{:S(2)}) copy-start(s32[128,4]{0,1:T(4,128)} %param.6) | copy-start | bytes 6148
  117.8 17.8 %all-to-all-start.1 = ((bf16[32,128,4,24]{1,3,2,0:T(8,128)(2,1)}), bf16[32,128,4,24]{1,3,2,0:T(8,128)(2,1)S(1)}, u32[]{:S(2)}, u32[]{:S(2)}) async-start(bf16[32,128,4,24]{1,3,2,0:T(8,128)(2,1)} %copy.25), calls=%async_computation.1 | async-start | bytes 1572864 | tf_op jit(solution)/shard_map/all_to_all | solution.py:50
  139.2 18.0 %all-to-all-start.2 = ((bf16[32,128,4,24]{1,3,2,0:T(8,128)(2,1)}), bf16[32,128,4,24]{1,3,2,0:T(8,128)(2,1)S(1)}, u32[]{:S(2)}, u32[]{:S(2)}) async-start(bf16[32,128,4,24]{1,3,2,0:T(8,128)(2,1)} %copy.29), calls=%async_computation.2 | async-start | bytes 1572864 | tf_op jit(solution)/shard_map/all_to_all | solution.py:34
  145.1 101.1 %reduce-scatter.2.cloned.1.call-start = ((), (), s32[]{:S(2)}) async-start(), calls=%async_computation.5 | async-start | bytes 1671168 | tf_op jit(solution)/shard_map/reduce_scatter | solution.py:58
  173.5 1.1 copy-start
Sparse Core Ops, SparseCore 0:
  11.1 92.4 all-gather.1
  173.6 72.4 reduce-scatter.1
